TPU v7x, 256 devices: a whole 4x4x8 slice. The times are simulated.
256 devices in a mesh: space: 16 (over x_hi, z), chan: 8 (over y, core), dp: 2 (over x_lo).
Axes of the slice: x: 4 (x_hi: 2, x_lo: 2; x = x_hi * 2 + x_lo), y: 4, z: 8, core: 2. Of those that a mesh axis runs over, the one named last changes fastest.
Arguments:
- inputs: bfloat16 [2, 32, 8, 128, 512], P('dp', 'space', None, 'chan'), may hold values from -6 to 6
- cotangent: bfloat16 [2, 32, 8, 128, 512], P('dp', 'space', None, 'chan'), may hold values from -6 to 6
- weight: bfloat16 [27, 128, 128], P(None, 'chan'), may hold values from -0.109375 to 0.109375
Outputs:
- input_grad: bfloat16 [2, 32, 8, 128, 512], P('dp', 'space', None, 'chan')
- weight_grad: float32 [27, 128, 128], P(None, 'chan')
All inputs are finite; a program needn't handle non-finite values.
Results may differ from a plain program's by a relative error of at most 0.001.
Values may be sent and summed in bfloat16 or wider, within the bound.
No kernel may reach another device: no remote copies, remote signals or barrier semaphores. Data moves between devices by JAX's collectives and lax.ppermute only.
A program may use at most 64 MiB of HBM per device.

v0:
```python
import math
import jax
import jax.numpy as jnp
from jax import lax
from jax.sharding import PartitionSpec as P


def from_behind(value, axis, steps):
    count = lax.axis_size(axis)
    initial, last = (max(0, -steps), min(count, count - steps))
    return lax.ppermute(value, axis, [(source, source + steps) for source in range(initial, last)])


def exchange_sum(value, axis, distance):
    count = lax.axis_size(axis)
    return value + lax.ppermute(value, axis, [(i, i ^ distance) for i in range(count)])


def butterfly_sum(value):
    value = exchange_sum(value, "dp", 1)
    for distance in (1, 8, 2, 4):
        value = exchange_sum(value, "space", distance)
    return value


def shift_cells(block, step_z, step_y):
    zero = jnp.zeros((), block.dtype)
    config = ((0, 0, 0), (0, 0, 0), (step_z, -step_z, 0), (0, 0, 0), (step_y, -step_y, 0))
    return lax.pad(block, zero, config)


def local(inputs, cotangent, weight):
    samples, planes, depth, channels, width = inputs.shape
    outputs = weight.shape[2]
    inputs_ext = jnp.concatenate(
        [from_behind(inputs[:, -1:], "space", 1), inputs, from_behind(inputs[:, :1], "space", -1)],
        axis=1,
    )
    gathered = lax.all_gather(cotangent, "chan", axis=3, tiled=True)
    stacked = jnp.concatenate(
        [
            shift_cells(inputs_ext, -step_z, -step_y)
            for step_z in (-1, 0, 1)
            for step_y in (-1, 0, 1)
        ],
        axis=3,
    )
    groups = []
    for step_x in (-1, 0, 1):
        source = stacked[:, 1 + step_x : 1 + step_x + planes]
        groups.append(
            jnp.einsum("bxzky,bxzcy->kc", source, gathered, preferred_element_type=jnp.float32)
        )
    local_grad = jnp.concatenate(groups, axis=0).reshape(27, channels, outputs)
    count = samples * lax.axis_size("dp") * planes * lax.axis_size("space") * depth * width
    scale = 1.0 / math.sqrt(count)
    weight_grad = butterfly_sum(local_grad) * scale
    contrib = {}
    for step_x in (-1, 0, 1):
        first = 9 * (step_x + 1)
        total = None
        for step_y in (-1, 0, 1):
            kernel = weight[first + step_y + 1 : first + 9 : 3].reshape(3 * channels, outputs)
            product = jnp.einsum(
                "bxzcy,kc->bxzky", gathered, kernel, preferred_element_type=jnp.float32
            )
            for place, step_z in enumerate((-1, 0, 1)):
                part = shift_cells(
                    product[:, :, :, place * channels : (place + 1) * channels], step_z, step_y
                )
                total = part if total is None else total + part
        contrib[step_x] = total
    from_prev = from_behind(contrib[1][:, -1:], "space", 1)
    from_next = from_behind(contrib[-1][:, :1], "space", -1)
    accum = (
        contrib[0]
        + jnp.concatenate([from_prev, contrib[1][:, : planes - 1]], axis=1)
        + jnp.concatenate([contrib[-1][:, 1:], from_next], axis=1)
    )
    input_grad = accum.astype(jnp.bfloat16)
    return (input_grad, weight_grad)


def solution(mesh):
    placed = (
        P("dp", "space", None, "chan", None),
        P("dp", "space", None, "chan", None),
        P(None, "chan", None),
    )
    return jax.shard_map(
        local,
        mesh=mesh,
        in_specs=placed,
        out_specs=(P("dp", "space", None, "chan", None), P(None, "chan", None)),
        check_vma=False,
    )
```

profile of v0, /device:TPU:96, one launch (start us, length us, event | category | flops | bytes accessed | tf_op | source)
XLA Modules:
  0.0 112.7 jit_solution(3024075588676889384)
XLA Ops:
  7.2 0.0 all-gather.2.cloned.1.call-start
  7.2 0.7 all-gather.2.cloned.1.call-update
  7.9 1.0 fusion.106
  8.9 5.0 %collective-permute-start.2 = (bf16[1,1,8,16,512]{4,3,2,1,0:T(8,128)(2,1)S(1)}, bf16[1,1,8,16,512]{4,3,2,1,0:T(8,128)(2,1)S(1)}, u32[]{:S(2)}, u32[]{:S(2)}) collective-permute-start(bf16[1,1,8,16,512]{4,3,2,1,0:T(8,128)(2,1)S(1)} %get-tuple-element.31), channel_id=1, source_target_pairs={{0,16},{16,32},{32,48},{48,64},{64,80},{80,96},{96,112},{112,128},... | collective-permute-start | bytes 393224 | tf_op jit(solution)/shard_map/ppermute | solution.py:11
  13.9 1.9 %collective-permute-start.3 = (bf16[1,1,8,16,512]{4,3,2,1,0:T(8,128)(2,1)S(1)}, bf16[1,1,8,16,512]{4,3,2,1,0:T(8,128)(2,1)S(1)}, u32[]{:S(2)}, u32[]{:S(2)}) collective-permute-start(bf16[1,1,8,16,512]{4,3,2,1,0:T(8,128)(2,1)S(1)} %get-tuple-element.30), channel_id=1, source_target_pairs={{16,0},{32,16},{48,32},{64,48},{80,64},{96,80},{112,96},{128,112},... | collective-permute-start | bytes 393224 | tf_op jit(solution)/shard_map/ppermute | solution.py:11
  15.9 0.9 fusion.107
  16.7 0.0 collective-permute-done.2
  16.8 1.0 constant_dynamic-update-slice_fusion.1
  17.7 4.3 %collective-permute-done.3 = bf16[1,1,8,16,512]{4,3,2,1,0:T(8,128)(2,1)S(1)} collective-permute-done((bf16[1,1,8,16,512]{4,3,2,1,0:T(8,128)(2,1)S(1)}, bf16[1,1,8,16,512]{4,3,2,1,0:T(8,128)(2,1)S(1)}, u32[]{:S(2)}, u32[]{:S(2)}) %collective-permute-start.3) | collective-permute-done | bytes 131104 | tf_op jit(solution)/shard_map/ppermute | solution.py:11
  22.0 0.0 copy-start.1
  22.0 1.0 fusion.91
  23.0 0.9 fusion.60
  23.9 1.1 fusion.92
  25.0 1.2 %fusion.83 = bf16[1,4,8,144,512]{4,3,2,1,0:T(8,128)(2,1)} fusion(bf16[1,4,8,144,512]{4,3,2,1,0:T(8,128)(2,1)} %fusion.92, bf16[1,4,8,16,512]{4,3,2,1,0:T(8,128)(2,1)S(1)} %constant_dynamic-update-slice_fusion), kind=kLoop, calls=%fused_computation.94 | loop fusion | bytes 1048576
  26.2 0.7 constant_dynamic-update-slice_fusion.5
  26.9 0.0 copy-done.1
  26.9 0.7 constant_dynamic-update-slice_fusion.4
  27.6 0.7 constant_dynamic-update-slice_fusion.3
  28.3 1.1 %fusion.84 = bf16[1,4,8,144,512]{4,3,2,1,0:T(8,128)(2,1)} fusion(bf16[1,4,8,144,512]{4,3,2,1,0:T(8,128)(2,1)} %constant_dynamic-update-slice_fusion.3, bf16[1,4,8,16,512]{4,3,2,1,0:T(8,128)(2,1)S(1)} %constant_dynamic-update-slice_fusion), kind=kLoop, calls=%fused_computation.95 | loop fusion | bytes 1048576
  29.4 1.0 fusion.93
  30.5 0.9 fusion.61
  31.4 1.1 fusion.94
  32.4 7.2 %all-gather.2.cloned.1.call-done = bf16[1,2,8,128,512]{4,3,2,1,0:T(8,128)(2,1)} async-done(((bf16[1,2,8,16,512]{4,3,2,1,0:T(8,128)(2,1)}), bf16[1,2,8,128,512]{4,3,2,1,0:T(8,128)(2,1)}) %all-gather.2.cloned.1.call-update) | async-done | bytes 2097168 | tf_op jit(solution)/shard_map/all_gather | solution.py:39
  39.6 0.0 copy-start
  39.6 3.2 %fusion.51 = f32[144,128]{1,0:T(8,128)S(1)} fusion(bf16[1,2,8,128,512]{4,3,2,1,0:T(8,128)(2,1)} %all-gather.2.cloned.1.call-done, bf16[1,4,8,144,512]{4,3,2,1,0:T(8,128)(2,1)} %fusion.94), kind=kOutput, calls=%fused_computation.36 | convolution fusion | flops 301989888 | bytes 4530176 | tf_op jit(solution)/shard_map/bxzky,bxzcy->kc/dot_general | solution.py:52
  42.8 0.0 copy-done
  42.8 2.4 %fusion.54 = f32[144,128]{1,0:T(8,128)S(1)} fusion(bf16[1,2,8,128,512]{4,3,2,1,0:T(8,128)(2,1)S(1)} %copy-done, bf16[1,4,8,144,512]{4,3,2,1,0:T(8,128)(2,1)} %fusion.94), kind=kOutput, calls=%fused_computation.37 | convolution fusion | flops 301989888 | bytes 4530176 | tf_op jit(solution)/shard_map/bxzky,bxzcy->kc/dot_general | solution.py:52
  45.3 2.4 %fusion.57 = f32[144,128]{1,0:T(8,128)S(1)} fusion(bf16[1,2,8,128,512]{4,3,2,1,0:T(8,128)(2,1)S(1)} %copy-done, bf16[1,4,8,144,512]{4,3,2,1,0:T(8,128)(2,1)} %fusion.94), kind=kOutput, calls=%fused_computation.38 | convolution fusion | flops 301989888 | bytes 4530176 | tf_op jit(solution)/shard_map/bxzky,bxzcy->kc/dot_general | solution.py:52
  47.7 1.6 %collective-permute-start.4 = (f32[27,16,128]{2,1,0:T(8,128)S(1)}, f32[27,16,128]{2,1,0:T(8,128)S(1)}, u32[]{:S(2)}, u32[]{:S(2)}) collective-permute-start(f32[27,16,128]{2,1,0:T(8,128)S(1)} %bitcast.167), channel_id=1, source_target_pairs={{0,1},{1,0},{2,3},{3,2},{4,5},{5,4},{6,7},{7,6},{8,9},{9,8},{10,11... | collective-permute-start | bytes 663560 | tf_op jit(solution)/shard_map/ppermute | solution.py:16
  49.3 0.4 fusion.45
  49.7 0.1 fusion.97
  49.8 0.4 fusion.42
  50.2 0.4 fusion.48
  50.7 0.6 fusion.95
  51.2 0.8 fusion.82
  52.1 2.4 %collective-permute-start.1 = (f32[1,1,8,16,512]{4,3,2,1,0:T(8,128)S(1)}, f32[1,1,8,16,512]{4,3,2,1,0:T(8,128)S(1)}, u32[]{:S(2)}, u32[]{:S(2)}) collective-permute-start(f32[1,1,8,16,512]{4,3,2,1,0:T(8,128)S(1)} %get-tuple-element.27), channel_id=1, source_target_pairs={{16,0},{32,16},{48,32},{64,48},{80,64},{96,80},{112,96},{128,112},... | collective-permute-start | bytes 786440 | tf_op jit(solution)/shard_map/ppermute | solution.py:11
  54.5 0.4 fusion.36
  54.9 0.1 fusion.100
  55.0 0.4 fusion.33
  55.4 0.4 fusion.39
  55.9 0.6 fusion.98
  56.4 0.8 fusion.76
  57.3 4.7 %collective-permute-start = (f32[1,1,8,16,512]{4,3,2,1,0:T(8,128)S(1)}, f32[1,1,8,16,512]{4,3,2,1,0:T(8,128)S(1)}, u32[]{:S(2)}, u32[]{:S(2)}) collective-permute-start(f32[1,1,8,16,512]{4,3,2,1,0:T(8,128)S(1)} %get-tuple-element.28), channel_id=1, source_target_pairs={{0,16},{16,32},{32,48},{48,64},{64,80},{80,96},{96,112},{112,128},... | collective-permute-start | bytes 786440 | tf_op jit(solution)/shard_map/ppermute | solution.py:11
  62.0 0.0 collective-permute-done.4
  62.0 0.1 collective-permute-start.5
  62.1 0.4 fusion.24
  62.6 0.4 fusion.30
  63.0 8.8 %collective-permute-done.5 = f32[27,16,128]{2,1,0:T(8,128)S(1)} collective-permute-done((f32[27,16,128]{2,1,0:T(8,128)S(1)}, f32[27,16,128]{2,1,0:T(8,128)S(1)}, u32[]{:S(2)}, u32[]{:S(2)}) %collective-permute-start.5) | collective-permute-done | bytes 221216 | tf_op jit(solution)/shard_map/ppermute | solution.py:16
  71.9 2.8 %collective-permute-start.6 = (f32[27,16,128]{2,1,0:T(8,128)S(1)}, f32[27,16,128]{2,1,0:T(8,128)S(1)}, u32[]{:S(2)}, u32[]{:S(2)}) collective-permute-start(f32[27,16,128]{2,1,0:T(8,128)S(1)} %add.184), channel_id=1, source_target_pairs={{0,128},{16,144},{32,160},{48,176},{64,192},{80,208},{96,224},{112... | collective-permute-start | bytes 663560 | tf_op jit(solution)/shard_map/ppermute | solution.py:16
  74.6 0.6 fusion.101
  75.2 0.4 fusion.27
  75.6 4.0 %collective-permute-done.6 = f32[27,16,128]{2,1,0:T(8,128)S(1)} collective-permute-done((f32[27,16,128]{2,1,0:T(8,128)S(1)}, f32[27,16,128]{2,1,0:T(8,128)S(1)}, u32[]{:S(2)}, u32[]{:S(2)}) %collective-permute-start.6) | collective-permute-done | bytes 221216 | tf_op jit(solution)/shard_map/ppermute | solution.py:16
  79.6 2.0 %collective-permute-start.7 = (f32[27,16,128]{2,1,0:T(8,128)S(1)}, f32[27,16,128]{2,1,0:T(8,128)S(1)}, u32[]{:S(2)}, u32[]{:S(2)}) collective-permute-start(f32[27,16,128]{2,1,0:T(8,128)S(1)} %add.185), channel_id=1, source_target_pairs={{0,32},{16,48},{32,0},{48,16},{64,96},{80,112},{96,64},{112,80},{1... | collective-permute-start | bytes 663560 | tf_op jit(solution)/shard_map/ppermute | solution.py:16
  81.7 0.1 fusion.103
  81.8 7.9 %collective-permute-done.7 = f32[27,16,128]{2,1,0:T(8,128)S(1)} collective-permute-done((f32[27,16,128]{2,1,0:T(8,128)S(1)}, f32[27,16,128]{2,1,0:T(8,128)S(1)}, u32[]{:S(2)}, u32[]{:S(2)}) %collective-permute-start.7) | collective-permute-done | bytes 221216 | tf_op jit(solution)/shard_map/ppermute | solution.py:16
  89.7 3.9 %collective-permute-start.8 = (f32[27,16,128]{2,1,0:T(8,128)S(1)}, f32[27,16,128]{2,1,0:T(8,128)S(1)}, u32[]{:S(2)}, u32[]{:S(2)}) collective-permute-start(f32[27,16,128]{2,1,0:T(8,128)S(1)} %add.186), channel_id=1, source_target_pairs={{0,64},{16,80},{32,96},{48,112},{64,0},{80,16},{96,32},{112,48},{1... | collective-permute-start | bytes 663560 | tf_op jit(solution)/shard_map/ppermute | solution.py:16
  93.7 0.0 collective-permute-done.1
  93.7 0.0 collective-permute-done
  93.7 1.5 %fusion.70 = bf16[1,2,8,16,512]{4,3,2,1,0:T(8,128)(2,1)} fusion(f32[1,2,8,16,512]{4,3,2,1,0:T(8,128)S(1)} %get-tuple-element.25, f32[1,2,8,16,512]{4,3,2,1,0:T(8,128)S(1)} %get-tuple-element.24, f32[1,2,8,16,512]{4,3,2,1,0:T(8,128)S(1)} %get-tuple-element.48, f32[1,2,8,16,512]{4,3,2,1,0:T(8,128)S(1)} %get-tuple-element.19, ...), kind=kLoop, calls=%fused_computation.81 | loop fusion | flops 1703936 | bytes 6029312 | tf_op jit(solution)/shard_map/convert_element_type | solution.py:80
  95.2 9.9 %collective-permute-done.8 = f32[27,16,128]{2,1,0:T(8,128)S(1)} collective-permute-done((f32[27,16,128]{2,1,0:T(8,128)S(1)}, f32[27,16,128]{2,1,0:T(8,128)S(1)}, u32[]{:S(2)}, u32[]{:S(2)}) %collective-permute-start.8) | collective-permute-done | bytes 221216 | tf_op jit(solution)/shard_map/ppermute | solution.py:16
  105.1 0.7 add_multiply_fusion
  (9 shorter events, 0.2 us)
Async XLA Ops:
  7.2 32.4 %all-gather.2.cloned.1.call-start = ((), (), s32[]{:S(2)}) async-start(), calls=%async_computation | async-start | bytes 2359296 | tf_op jit(solution)/shard_map/all_gather | solution.py:39
  8.9 7.8 %collective-permute-start.2 = (bf16[1,1,8,16,512]{4,3,2,1,0:T(8,128)(2,1)S(1)}, bf16[1,1,8,16,512]{4,3,2,1,0:T(8,128)(2,1)S(1)}, u32[]{:S(2)}, u32[]{:S(2)}) collective-permute-start(bf16[1,1,8,16,512]{4,3,2,1,0:T(8,128)(2,1)S(1)} %get-tuple-element.31), channel_id=1, source_target_pairs={{0,16},{16,32},{32,48},{48,64},{64,80},{80,96},{96,112},{112,128},... | collective-permute-start | bytes 393224 | tf_op jit(solution)/shard_map/ppermute | solution.py:11
  13.9 8.1 %collective-permute-start.3 = (bf16[1,1,8,16,512]{4,3,2,1,0:T(8,128)(2,1)S(1)}, bf16[1,1,8,16,512]{4,3,2,1,0:T(8,128)(2,1)S(1)}, u32[]{:S(2)}, u32[]{:S(2)}) collective-permute-start(bf16[1,1,8,16,512]{4,3,2,1,0:T(8,128)(2,1)S(1)} %get-tuple-element.30), channel_id=1, source_target_pairs={{16,0},{32,16},{48,32},{64,48},{80,64},{96,80},{112,96},{128,112},... | collective-permute-start | bytes 393224 | tf_op jit(solution)/shard_map/ppermute | solution.py:11
  22.0 4.8 %copy-start.1 = (bf16[1,2,8,16,512]{4,3,2,1,0:T(8,128)(2,1)S(1)}, bf16[1,2,8,16,512]{4,3,2,1,0:T(8,128)(2,1)}, u32[]{:S(2)}) copy-start(bf16[1,2,8,16,512]{4,3,2,1,0:T(8,128)(2,1)} %param.3) | copy-start | bytes 786436
  39.6 3.2 %copy-start = (bf16[1,2,8,128,512]{4,3,2,1,0:T(8,128)(2,1)S(1)}, bf16[1,2,8,128,512]{4,3,2,1,0:T(8,128)(2,1)}, u32[]{:S(2)}) copy-start(bf16[1,2,8,128,512]{4,3,2,1,0:T(8,128)(2,1)} %all-gather.2.cloned.1.call-done) | copy-start | bytes 6291460
  47.7 14.3 %collective-permute-start.4 = (f32[27,16,128]{2,1,0:T(8,128)S(1)}, f32[27,16,128]{2,1,0:T(8,128)S(1)}, u32[]{:S(2)}, u32[]{:S(2)}) collective-permute-start(f32[27,16,128]{2,1,0:T(8,128)S(1)} %bitcast.167), channel_id=1, source_target_pairs={{0,1},{1,0},{2,3},{3,2},{4,5},{5,4},{6,7},{7,6},{8,9},{9,8},{10,11... | collective-permute-start | bytes 663560 | tf_op jit(solution)/shard_map/ppermute | solution.py:16
  52.1 41.6 %collective-permute-start.1 = (f32[1,1,8,16,512]{4,3,2,1,0:T(8,128)S(1)}, f32[1,1,8,16,512]{4,3,2,1,0:T(8,128)S(1)}, u32[]{:S(2)}, u32[]{:S(2)}) collective-permute-start(f32[1,1,8,16,512]{4,3,2,1,0:T(8,128)S(1)} %get-tuple-element.27), channel_id=1, source_target_pairs={{16,0},{32,16},{48,32},{64,48},{80,64},{96,80},{112,96},{128,112},... | collective-permute-start | bytes 786440 | tf_op jit(solution)/shard_map/ppermute | solution.py:11
  57.3 36.4 %collective-permute-start = (f32[1,1,8,16,512]{4,3,2,1,0:T(8,128)S(1)}, f32[1,1,8,16,512]{4,3,2,1,0:T(8,128)S(1)}, u32[]{:S(2)}, u32[]{:S(2)}) collective-permute-start(f32[1,1,8,16,512]{4,3,2,1,0:T(8,128)S(1)} %get-tuple-element.28), channel_id=1, source_target_pairs={{0,16},{16,32},{32,48},{48,64},{64,80},{80,96},{96,112},{112,128},... | collective-permute-start | bytes 786440 | tf_op jit(solution)/shard_map/ppermute | solution.py:11
  62.0 9.8 %collective-permute-start.5 = (f32[27,16,128]{2,1,0:T(8,128)S(1)}, f32[27,16,128]{2,1,0:T(8,128)S(1)}, u32[]{:S(2)}, u32[]{:S(2)}) collective-permute-start(f32[27,16,128]{2,1,0:T(8,128)S(1)} %add.183), channel_id=1, source_target_pairs={{0,16},{16,0},{32,48},{48,32},{64,80},{80,64},{96,112},{112,96},{1... | collective-permute-start | bytes 663560 | tf_op jit(solution)/shard_map/ppermute | solution.py:16
  71.9 7.7 %collective-permute-start.6 = (f32[27,16,128]{2,1,0:T(8,128)S(1)}, f32[27,16,128]{2,1,0:T(8,128)S(1)}, u32[]{:S(2)}, u32[]{:S(2)}) collective-permute-start(f32[27,16,128]{2,1,0:T(8,128)S(1)} %add.184), channel_id=1, source_target_pairs={{0,128},{16,144},{32,160},{48,176},{64,192},{80,208},{96,224},{112... | collective-permute-start | bytes 663560 | tf_op jit(solution)/shard_map/ppermute | solution.py:16
  79.6 10.1 %collective-permute-start.7 = (f32[27,16,128]{2,1,0:T(8,128)S(1)}, f32[27,16,128]{2,1,0:T(8,128)S(1)}, u32[]{:S(2)}, u32[]{:S(2)}) collective-permute-start(f32[27,16,128]{2,1,0:T(8,128)S(1)} %add.185), channel_id=1, source_target_pairs={{0,32},{16,48},{32,0},{48,16},{64,96},{80,112},{96,64},{112,80},{1... | collective-permute-start | bytes 663560 | tf_op jit(solution)/shard_map/ppermute | solution.py:16
  89.7 15.4 %collective-permute-start.8 = (f32[27,16,128]{2,1,0:T(8,128)S(1)}, f32[27,16,128]{2,1,0:T(8,128)S(1)}, u32[]{:S(2)}, u32[]{:S(2)}) collective-permute-start(f32[27,16,128]{2,1,0:T(8,128)S(1)} %add.186), channel_id=1, source_target_pairs={{0,64},{16,80},{32,96},{48,112},{64,0},{80,16},{96,32},{112,48},{1... | collective-permute-start | bytes 663560 | tf_op jit(solution)/shard_map/ppermute | solution.py:16
Sparse Core Ops, SparseCore 0:
  9.8 29.7 all-gather.1
where the time goes:
time: 113 us
  waiting for transfers between devices  42.8 us (38%)
  starting transfers between devices  24.4 us (22%)
  local copies, waits for them, and re-layouts  15.3 us (14%)
  between operations  14.3 us (13%)
  matrix products  11.9 us (11%)
  other arithmetic  4 us (4%)
    ppermute x5, waiting for transfers between devices, exchange_sum(): lax.ppermute(value, axis, [(i, i ^ distance) for i in range(count)])  30.7 us
    ppermute x4, starting transfers between devices, from_behind(): lax.ppermute(value, axis, [(source, source + steps) for source in range(i...  14 us
    ppermute x5, starting transfers between devices, exchange_sum(): lax.ppermute(value, axis, [(i, i ^ distance) for i in range(count)])  10.4 us
    unnamed x16, local copies, waits for them, and re-layouts  10.3 us
    dot_general x3, matrix products, local(): jnp.einsum('bxzky,bxzcy->kc', source, gathered, preferred_element_type=jn...  8.07 us
    all_gather x1, waiting for transfers between devices, local(): gathered = lax.all_gather(cotangent, 'chan', axis=3, tiled=True)  7.18 us
    ppermute x4, waiting for transfers between devices, from_behind(): lax.ppermute(value, axis, [(source, source + steps) for source in range(i...  4.29 us
    dot_general x9, matrix products, local(): jnp.einsum('bxzcy,kc->bxzky', gathered, kernel, preferred_element_type=jn...  3.81 us
  transfers between devices with their start and end apart: 10, of which 6 were waited for; matrix products, arithmetic and copies ran while one was open for 20% of the time, Pallas kernels for 0%

commit v1 on v0

--- a/solution.py
+++ b/solution.py
@@ -3,6 +3,19 @@
 import jax.numpy as jnp
 from jax import lax
 from jax.sharding import PartitionSpec as P
+
+
+def ring_gather(x, axis, dim):
+    ways = lax.axis_size(axis)
+    up = [(d, (d + 1) % ways) for d in range(ways)]
+    down = [(d, (d - 1) % ways) for d in range(ways)]
+    earlier, later = ([x], [x])
+    for _ in range(ways // 2):
+        earlier.append(lax.ppermute(earlier[-1], axis, up))
+    for _ in range((ways - 1) // 2):
+        later.append(lax.ppermute(later[-1], axis, down))
+    line = jnp.concatenate([*earlier[::-1], *later[1:]], axis=dim)
+    return jnp.roll(line, (lax.axis_index(axis) - ways // 2) * x.shape[dim], axis=dim)
 
 
 def from_behind(value, axis, steps):
@@ -36,7 +49,7 @@
         [from_behind(inputs[:, -1:], "space", 1), inputs, from_behind(inputs[:, :1], "space", -1)],
         axis=1,
     )
-    gathered = lax.all_gather(cotangent, "chan", axis=3, tiled=True)
+    gathered = ring_gather(cotangent, "chan", 3)
     stacked = jnp.concatenate(
         [
             shift_cells(inputs_ext, -step_z, -step_y)

time: 113 us -> 102 us (0.903)
  the two profiles are of different devices: /device:TPU:96 before, /device:TPU:8 now
where the time goes in v1:
time: 102 us; the launch traced here: 101 us
  waiting for transfers between devices  51.1 us (50%)
  starting transfers between devices  32 us (31%)
  local copies, waits for them, and re-layouts  6.89 us (7%)
  matrix products  6.1 us (6%)
  other arithmetic  3.99 us (4%)
  between operations  1.11 us (1%)
    ppermute x5, waiting for transfers between devices, exchange_sum(): lax.ppermute(value, axis, [(i, i ^ distance) for i in range(count)])  34.6 us
    ppermute x5, starting transfers between devices, exchange_sum(): lax.ppermute(value, axis, [(i, i ^ distance) for i in range(count)])  15.6 us
    ppermute x4, waiting for transfers between devices, ring_gather(): earlier.append(lax.ppermute(earlier[-1], axis, up))  12.2 us
    ppermute x4, starting transfers between devices, from_behind(): lax.ppermute(value, axis, [(source, source + steps) for source in range(i...  11 us
    ppermute x3, starting transfers between devices, ring_gather(): later.append(lax.ppermute(later[-1], axis, down))  5.37 us
    ppermute x4, waiting for transfers between devices, from_behind(): lax.ppermute(value, axis, [(source, source + steps) for source in range(i...  3.98 us
    dot_general x9, matrix products, local(): jnp.einsum('bxzcy,kc->bxzky', gathered, kernel, preferred_element_type=jn...  3.79 us
    unnamed x31, local copies, waits for them, and re-layouts  2.69 us
  transfers between devices with their start and end apart: 16, of which 10 were waited for; matrix products, arithmetic and copies ran while one was open for 14% of the time, Pallas kernels for 0%

profile of v1, /device:TPU:8, one launch (start us, length us, event | category | flops | bytes accessed | tf_op | source)
XLA Modules:
  0.0 101.2 jit_solution(11319920972530246695)
XLA Ops:
  0.6 0.0 copy-start
  0.6 0.0 collective-permute-start
  0.7 1.7 %collective-permute-start.4 = (bf16[1,2,8,16,512]{4,3,2,1,0:T(8,128)(2,1)}, bf16[1,2,8,16,512]{4,3,2,1,0:T(8,128)(2,1)S(1)}, u32[]{:S(2)}, u32[]{:S(2)}) collective-permute-start(bf16[1,2,8,16,512]{4,3,2,1,0:T(8,128)(2,1)} %param.4), channel_id=1, source_target_pairs={{0,14},{2,0},{4,2},{6,4},{8,6},{10,8},{12,10},{14,12},{1,15},{3,1}... | collective-permute-start | bytes 786440 | tf_op jit(solution)/shard_map/ppermute | solution.py:16
  2.4 1.0 fusion.106
  3.4 3.8 %collective-permute-start.9 = (bf16[1,1,8,16,512]{4,3,2,1,0:T(8,128)(2,1)S(1)}, bf16[1,1,8,16,512]{4,3,2,1,0:T(8,128)(2,1)S(1)}, u32[]{:S(2)}, u32[]{:S(2)}) collective-permute-start(bf16[1,1,8,16,512]{4,3,2,1,0:T(8,128)(2,1)S(1)} %get-tuple-element.31), channel_id=1, source_target_pairs={{0,16},{16,32},{32,48},{48,64},{64,80},{80,96},{96,112},{112,128},... | collective-permute-start | bytes 393224 | tf_op jit(solution)/shard_map/ppermute | solution.py:24
  7.2 1.3 %collective-permute-start.10 = (bf16[1,1,8,16,512]{4,3,2,1,0:T(8,128)(2,1)S(1)}, bf16[1,1,8,16,512]{4,3,2,1,0:T(8,128)(2,1)S(1)}, u32[]{:S(2)}, u32[]{:S(2)}) collective-permute-start(bf16[1,1,8,16,512]{4,3,2,1,0:T(8,128)(2,1)S(1)} %get-tuple-element.30), channel_id=1, source_target_pairs={{16,0},{32,16},{48,32},{64,48},{80,64},{96,80},{112,96},{128,112},... | collective-permute-start | bytes 393224 | tf_op jit(solution)/shard_map/ppermute | solution.py:24
  8.5 0.9 fusion.107
  9.4 0.7 collective-permute-done.9
  10.1 1.0 constant_dynamic-update-slice_fusion.17
  11.1 3.3 %collective-permute-done.10 = bf16[1,1,8,16,512]{4,3,2,1,0:T(8,128)(2,1)S(1)} collective-permute-done((bf16[1,1,8,16,512]{4,3,2,1,0:T(8,128)(2,1)S(1)}, bf16[1,1,8,16,512]{4,3,2,1,0:T(8,128)(2,1)S(1)}, u32[]{:S(2)}, u32[]{:S(2)}) %collective-permute-start.10) | collective-permute-done | bytes 131104 | tf_op jit(solution)/shard_map/ppermute | solution.py:24
  14.4 0.2 fusion.91
  14.6 0.0 collective-permute-done
  14.7 0.0 collective-permute-start.1
  14.7 0.2 fusion.92
  14.9 0.0 copy-start.1
  14.9 0.3 fusion.83
  15.3 5.2 %collective-permute-done.1 = bf16[1,2,8,16,512]{4,3,2,1,0:T(8,128)(2,1)S(1)} collective-permute-done((bf16[1,2,8,16,512]{4,3,2,1,0:T(8,128)(2,1)S(1)}, bf16[1,2,8,16,512]{4,3,2,1,0:T(8,128)(2,1)S(1)}, u32[]{:S(2)}, u32[]{:S(2)}) %collective-permute-start.1) | collective-permute-done | bytes 262176 | tf_op jit(solution)/shard_map/ppermute | solution.py:14
  20.5 0.0 collective-permute-start.2
  20.5 0.3 fusion.84
  20.8 0.0 collective-permute-done.4
  20.8 1.8 %collective-permute-start.5 = (bf16[1,2,8,16,512]{4,3,2,1,0:T(8,128)(2,1)S(1)}, bf16[1,2,8,16,512]{4,3,2,1,0:T(8,128)(2,1)S(1)}, u32[]{:S(2)}, u32[]{:S(2)}) collective-permute-start(bf16[1,2,8,16,512]{4,3,2,1,0:T(8,128)(2,1)S(1)} %collective-permute-done.4), channel_id=1, source_target_pairs={{0,14},{2,0},{4,2},{6,4},{8,6},{10,8},{12,10},{14,12},{1,15},{3,1}... | collective-permute-start | bytes 786440 | tf_op jit(solution)/shard_map/ppermute | solution.py:16
  22.6 3.7 %collective-permute-done.2 = bf16[1,2,8,16,512]{4,3,2,1,0:T(8,128)(2,1)S(1)} collective-permute-done((bf16[1,2,8,16,512]{4,3,2,1,0:T(8,128)(2,1)S(1)}, bf16[1,2,8,16,512]{4,3,2,1,0:T(8,128)(2,1)S(1)}, u32[]{:S(2)}, u32[]{:S(2)}) %collective-permute-start.2) | collective-permute-done | bytes 262176 | tf_op jit(solution)/shard_map/ppermute | solution.py:14
  26.3 0.0 collective-permute-start.3
  26.3 0.2 fusion.93
  26.5 0.2 fusion.94
  26.8 0.0 collective-permute-done.5
  26.8 1.9 %collective-permute-start.6 = (bf16[1,2,8,16,512]{4,3,2,1,0:T(8,128)(2,1)S(1)}, bf16[1,2,8,16,512]{4,3,2,1,0:T(8,128)(2,1)S(1)}, u32[]{:S(2)}, u32[]{:S(2)}) collective-permute-start(bf16[1,2,8,16,512]{4,3,2,1,0:T(8,128)(2,1)S(1)} %collective-permute-done.5), channel_id=1, source_target_pairs={{0,14},{2,0},{4,2},{6,4},{8,6},{10,8},{12,10},{14,12},{1,15},{3,1}... | collective-permute-start | bytes 786440 | tf_op jit(solution)/shard_map/ppermute | solution.py:16
  28.7 3.4 %collective-permute-done.3 = bf16[1,2,8,16,512]{4,3,2,1,0:T(8,128)(2,1)S(1)} collective-permute-done((bf16[1,2,8,16,512]{4,3,2,1,0:T(8,128)(2,1)S(1)}, bf16[1,2,8,16,512]{4,3,2,1,0:T(8,128)(2,1)S(1)}, u32[]{:S(2)}, u32[]{:S(2)}) %collective-permute-start.3) | collective-permute-done | bytes 262176 | tf_op jit(solution)/shard_map/ppermute | solution.py:14
  32.3 0.3 collective-permute-done.6
  32.8 0.8 fusion.51
  33.6 0.8 fusion.54
  34.4 0.8 fusion.57
  35.2 1.6 %collective-permute-start.11 = (f32[27,16,128]{2,1,0:T(8,128)S(1)}, f32[27,16,128]{2,1,0:T(8,128)S(1)}, u32[]{:S(2)}, u32[]{:S(2)}) collective-permute-start(f32[27,16,128]{2,1,0:T(8,128)S(1)} %bitcast.185), channel_id=1, source_target_pairs={{0,1},{1,0},{2,3},{3,2},{4,5},{5,4},{6,7},{7,6},{8,9},{9,8},{10,11... | collective-permute-start | bytes 663560 | tf_op jit(solution)/shard_map/ppermute | solution.py:29
  36.8 0.4 fusion.24
  37.2 0.4 fusion.30
  37.6 0.4 fusion.27
  38.0 0.1 fusion.97
  38.1 0.6 fusion.95
  38.7 0.8 fusion.82
  39.6 1.3 %collective-permute-start.8 = (f32[1,1,8,16,512]{4,3,2,1,0:T(8,128)S(1)}, f32[1,1,8,16,512]{4,3,2,1,0:T(8,128)S(1)}, u32[]{:S(2)}, u32[]{:S(2)}) collective-permute-start(f32[1,1,8,16,512]{4,3,2,1,0:T(8,128)S(1)} %get-tuple-element.27), channel_id=1, source_target_pairs={{16,0},{32,16},{48,32},{64,48},{80,64},{96,80},{112,96},{128,112},... | collective-permute-start | bytes 786440 | tf_op jit(solution)/shard_map/ppermute | solution.py:24
  40.9 0.4 fusion.33
  41.3 0.4 fusion.39
  41.7 0.4 fusion.36
  42.1 0.1 fusion.100
  42.3 0.6 fusion.98
  42.8 0.8 fusion.76
  43.7 4.6 %collective-permute-start.7 = (f32[1,1,8,16,512]{4,3,2,1,0:T(8,128)S(1)}, f32[1,1,8,16,512]{4,3,2,1,0:T(8,128)S(1)}, u32[]{:S(2)}, u32[]{:S(2)}) collective-permute-start(f32[1,1,8,16,512]{4,3,2,1,0:T(8,128)S(1)} %get-tuple-element.28), channel_id=1, source_target_pairs={{0,16},{16,32},{32,48},{48,64},{64,80},{80,96},{96,112},{112,128},... | collective-permute-start | bytes 786440 | tf_op jit(solution)/shard_map/ppermute | solution.py:24
  48.3 0.0 collective-permute-done.11
  48.3 3.1 %collective-permute-start.12 = (f32[27,16,128]{2,1,0:T(8,128)S(1)}, f32[27,16,128]{2,1,0:T(8,128)S(1)}, u32[]{:S(2)}, u32[]{:S(2)}) collective-permute-start(f32[27,16,128]{2,1,0:T(8,128)S(1)} %add.196), channel_id=1, source_target_pairs={{0,16},{16,0},{32,48},{48,32},{64,80},{80,64},{96,112},{112,96},{1... | collective-permute-start | bytes 663560 | tf_op jit(solution)/shard_map/ppermute | solution.py:29
  51.4 0.4 fusion.42
  51.8 0.4 fusion.48
  52.3 7.3 %collective-permute-done.12 = f32[27,16,128]{2,1,0:T(8,128)S(1)} collective-permute-done((f32[27,16,128]{2,1,0:T(8,128)S(1)}, f32[27,16,128]{2,1,0:T(8,128)S(1)}, u32[]{:S(2)}, u32[]{:S(2)}) %collective-permute-start.12) | collective-permute-done | bytes 221216 | tf_op jit(solution)/shard_map/ppermute | solution.py:29
  59.6 8.6 %collective-permute-start.13 = (f32[27,16,128]{2,1,0:T(8,128)S(1)}, f32[27,16,128]{2,1,0:T(8,128)S(1)}, u32[]{:S(2)}, u32[]{:S(2)}) collective-permute-start(f32[27,16,128]{2,1,0:T(8,128)S(1)} %add.197), channel_id=1, source_target_pairs={{0,128},{16,144},{32,160},{48,176},{64,192},{80,208},{96,224},{112... | collective-permute-start | bytes 663560 | tf_op jit(solution)/shard_map/ppermute | solution.py:29
  68.2 0.6 fusion.101
  68.8 0.4 fusion.45
  69.2 4.9 %collective-permute-done.13 = f32[27,16,128]{2,1,0:T(8,128)S(1)} collective-permute-done((f32[27,16,128]{2,1,0:T(8,128)S(1)}, f32[27,16,128]{2,1,0:T(8,128)S(1)}, u32[]{:S(2)}, u32[]{:S(2)}) %collective-permute-start.13) | collective-permute-done | bytes 221216 | tf_op jit(solution)/shard_map/ppermute | solution.py:29
  74.1 0.1 collective-permute-start.14
  74.3 0.1 fusion.103
  74.4 12.5 %collective-permute-done.14 = f32[27,16,128]{2,1,0:T(8,128)S(1)} collective-permute-done((f32[27,16,128]{2,1,0:T(8,128)S(1)}, f32[27,16,128]{2,1,0:T(8,128)S(1)}, u32[]{:S(2)}, u32[]{:S(2)}) %collective-permute-start.14) | collective-permute-done | bytes 221216 | tf_op jit(solution)/shard_map/ppermute | solution.py:29
  87.0 2.2 %collective-permute-start.15 = (f32[27,16,128]{2,1,0:T(8,128)S(1)}, f32[27,16,128]{2,1,0:T(8,128)S(1)}, u32[]{:S(2)}, u32[]{:S(2)}) collective-permute-start(f32[27,16,128]{2,1,0:T(8,128)S(1)} %add.199), channel_id=1, source_target_pairs={{0,64},{16,80},{32,96},{48,112},{64,0},{80,16},{96,32},{112,48},{1... | collective-permute-start | bytes 663560 | tf_op jit(solution)/shard_map/ppermute | solution.py:29
  89.1 0.0 collective-permute-done.8
  89.1 1.5 %fusion.70 = bf16[1,2,8,16,512]{4,3,2,1,0:T(8,128)(2,1)} fusion(f32[1,2,8,16,512]{4,3,2,1,0:T(8,128)S(1)} %get-tuple-element.25, f32[1,2,8,16,512]{4,3,2,1,0:T(8,128)S(1)} %get-tuple-element.24, f32[1,2,8,16,512]{4,3,2,1,0:T(8,128)S(1)} %get-tuple-element.48, f32[1,2,8,16,512]{4,3,2,1,0:T(8,128)S(1)} %get-tuple-element.19, ...), kind=kLoop, calls=%fused_computation.81 | loop fusion | flops 1703936 | bytes 6029312 | tf_op jit(solution)/shard_map/convert_element_type | solution.py:93
  90.6 9.9 %collective-permute-done.15 = f32[27,16,128]{2,1,0:T(8,128)S(1)} collective-permute-done((f32[27,16,128]{2,1,0:T(8,128)S(1)}, f32[27,16,128]{2,1,0:T(8,128)S(1)}, u32[]{:S(2)}, u32[]{:S(2)}) %collective-permute-start.15) | collective-permute-done | bytes 221216 | tf_op jit(solution)/shard_map/ppermute | solution.py:29
  100.5 0.7 add_multiply_fusion
  (33 shorter events, 0.7 us)
Async XLA Ops:
  0.6 19.8 %copy-start = (bf16[1,2,8,16,512]{4,3,2,1,0:T(8,128)(2,1)S(1)}, bf16[1,2,8,16,512]{4,3,2,1,0:T(8,128)(2,1)}, u32[]{:S(2)}) copy-start(bf16[1,2,8,16,512]{4,3,2,1,0:T(8,128)(2,1)} %param.3) | copy-start | bytes 786436
  0.6 14.0 %collective-permute-start = (bf16[1,2,8,16,512]{4,3,2,1,0:T(8,128)(2,1)}, bf16[1,2,8,16,512]{4,3,2,1,0:T(8,128)(2,1)S(1)}, u32[]{:S(2)}, u32[]{:S(2)}) collective-permute-start(bf16[1,2,8,16,512]{4,3,2,1,0:T(8,128)(2,1)} %param.4), channel_id=1, source_target_pairs={{0,2},{2,4},{4,6},{6,8},{8,10},{10,12},{12,14},{14,0},{1,3},{3,5},... | collective-permute-start | bytes 786440 | tf_op jit(solution)/shard_map/ppermute | solution.py:14
  0.7 20.2 %collective-permute-start.4 = (bf16[1,2,8,16,512]{4,3,2,1,0:T(8,128)(2,1)}, bf16[1,2,8,16,512]{4,3,2,1,0:T(8,128)(2,1)S(1)}, u32[]{:S(2)}, u32[]{:S(2)}) collective-permute-start(bf16[1,2,8,16,512]{4,3,2,1,0:T(8,128)(2,1)} %param.4), channel_id=1, source_target_pairs={{0,14},{2,0},{4,2},{6,4},{8,6},{10,8},{12,10},{14,12},{1,15},{3,1}... | collective-permute-start | bytes 786440 | tf_op jit(solution)/shard_map/ppermute | solution.py:16
  3.4 6.7 %collective-permute-start.9 = (bf16[1,1,8,16,512]{4,3,2,1,0:T(8,128)(2,1)S(1)}, bf16[1,1,8,16,512]{4,3,2,1,0:T(8,128)(2,1)S(1)}, u32[]{:S(2)}, u32[]{:S(2)}) collective-permute-start(bf16[1,1,8,16,512]{4,3,2,1,0:T(8,128)(2,1)S(1)} %get-tuple-element.31), channel_id=1, source_target_pairs={{0,16},{16,32},{32,48},{48,64},{64,80},{80,96},{96,112},{112,128},... | collective-permute-start | bytes 393224 | tf_op jit(solution)/shard_map/ppermute | solution.py:24
  7.2 7.1 %collective-permute-start.10 = (bf16[1,1,8,16,512]{4,3,2,1,0:T(8,128)(2,1)S(1)}, bf16[1,1,8,16,512]{4,3,2,1,0:T(8,128)(2,1)S(1)}, u32[]{:S(2)}, u32[]{:S(2)}) collective-permute-start(bf16[1,1,8,16,512]{4,3,2,1,0:T(8,128)(2,1)S(1)} %get-tuple-element.30), channel_id=1, source_target_pairs={{16,0},{32,16},{48,32},{64,48},{80,64},{96,80},{112,96},{128,112},... | collective-permute-start | bytes 393224 | tf_op jit(solution)/shard_map/ppermute | solution.py:24
  14.7 5.8 %collective-permute-start.1 = (bf16[1,2,8,16,512]{4,3,2,1,0:T(8,128)(2,1)S(1)}, bf16[1,2,8,16,512]{4,3,2,1,0:T(8,128)(2,1)S(1)}, u32[]{:S(2)}, u32[]{:S(2)}) collective-permute-start(bf16[1,2,8,16,512]{4,3,2,1,0:T(8,128)(2,1)S(1)} %collective-permute-done), channel_id=1, source_target_pairs={{0,2},{2,4},{4,6},{6,8},{8,10},{10,12},{12,14},{14,0},{1,3},{3,5},... | collective-permute-start | bytes 786440 | tf_op jit(solution)/shard_map/ppermute | solution.py:14
  14.9 17.2 %copy-start.1 = (bf16[1,2,8,16,512]{4,3,2,1,0:T(8,128)(2,1)S(1)}, bf16[1,2,8,16,512]{4,3,2,1,0:T(8,128)(2,1)}, u32[]{:S(2)}) copy-start(bf16[1,2,8,16,512]{4,3,2,1,0:T(8,128)(2,1)} %param.4) | copy-start | bytes 786436
  20.5 5.8 %collective-permute-start.2 = (bf16[1,2,8,16,512]{4,3,2,1,0:T(8,128)(2,1)S(1)}, bf16[1,2,8,16,512]{4,3,2,1,0:T(8,128)(2,1)S(1)}, u32[]{:S(2)}, u32[]{:S(2)}) collective-permute-start(bf16[1,2,8,16,512]{4,3,2,1,0:T(8,128)(2,1)S(1)} %collective-permute-done.1), channel_id=1, source_target_pairs={{0,2},{2,4},{4,6},{6,8},{8,10},{10,12},{12,14},{14,0},{1,3},{3,5},... | collective-permute-start | bytes 786440 | tf_op jit(solution)/shard_map/ppermute | solution.py:14
  20.8 6.0 %collective-permute-start.5 = (bf16[1,2,8,16,512]{4,3,2,1,0:T(8,128)(2,1)S(1)}, bf16[1,2,8,16,512]{4,3,2,1,0:T(8,128)(2,1)S(1)}, u32[]{:S(2)}, u32[]{:S(2)}) collective-permute-start(bf16[1,2,8,16,512]{4,3,2,1,0:T(8,128)(2,1)S(1)} %collective-permute-done.4), channel_id=1, source_target_pairs={{0,14},{2,0},{4,2},{6,4},{8,6},{10,8},{12,10},{14,12},{1,15},{3,1}... | collective-permute-start | bytes 786440 | tf_op jit(solution)/shard_map/ppermute | solution.py:16
  26.3 5.8 %collective-permute-start.3 = (bf16[1,2,8,16,512]{4,3,2,1,0:T(8,128)(2,1)S(1)}, bf16[1,2,8,16,512]{4,3,2,1,0:T(8,128)(2,1)S(1)}, u32[]{:S(2)}, u32[]{:S(2)}) collective-permute-start(bf16[1,2,8,16,512]{4,3,2,1,0:T(8,128)(2,1)S(1)} %collective-permute-done.2), channel_id=1, source_target_pairs={{0,2},{2,4},{4,6},{6,8},{8,10},{10,12},{12,14},{14,0},{1,3},{3,5},... | collective-permute-start | bytes 786440 | tf_op jit(solution)/shard_map/ppermute | solution.py:14
  26.8 5.8 %collective-permute-start.6 = (bf16[1,2,8,16,512]{4,3,2,1,0:T(8,128)(2,1)S(1)}, bf16[1,2,8,16,512]{4,3,2,1,0:T(8,128)(2,1)S(1)}, u32[]{:S(2)}, u32[]{:S(2)}) collective-permute-start(bf16[1,2,8,16,512]{4,3,2,1,0:T(8,128)(2,1)S(1)} %collective-permute-done.5), channel_id=1, source_target_pairs={{0,14},{2,0},{4,2},{6,4},{8,6},{10,8},{12,10},{14,12},{1,15},{3,1}... | collective-permute-start | bytes 786440 | tf_op jit(solution)/shard_map/ppermute | solution.py:16
  35.2 13.1 %collective-permute-start.11 = (f32[27,16,128]{2,1,0:T(8,128)S(1)}, f32[27,16,128]{2,1,0:T(8,128)S(1)}, u32[]{:S(2)}, u32[]{:S(2)}) collective-permute-start(f32[27,16,128]{2,1,0:T(8,128)S(1)} %bitcast.185), channel_id=1, source_target_pairs={{0,1},{1,0},{2,3},{3,2},{4,5},{5,4},{6,7},{7,6},{8,9},{9,8},{10,11... | collective-permute-start | bytes 663560 | tf_op jit(solution)/shard_map/ppermute | solution.py:29
  39.6 49.5 %collective-permute-start.8 = (f32[1,1,8,16,512]{4,3,2,1,0:T(8,128)S(1)}, f32[1,1,8,16,512]{4,3,2,1,0:T(8,128)S(1)}, u32[]{:S(2)}, u32[]{:S(2)}) collective-permute-start(f32[1,1,8,16,512]{4,3,2,1,0:T(8,128)S(1)} %get-tuple-element.27), channel_id=1, source_target_pairs={{16,0},{32,16},{48,32},{64,48},{80,64},{96,80},{112,96},{128,112},... | collective-permute-start | bytes 786440 | tf_op jit(solution)/shard_map/ppermute | solution.py:24
  43.7 45.4 %collective-permute-start.7 = (f32[1,1,8,16,512]{4,3,2,1,0:T(8,128)S(1)}, f32[1,1,8,16,512]{4,3,2,1,0:T(8,128)S(1)}, u32[]{:S(2)}, u32[]{:S(2)}) collective-permute-start(f32[1,1,8,16,512]{4,3,2,1,0:T(8,128)S(1)} %get-tuple-element.28), channel_id=1, source_target_pairs={{0,16},{16,32},{32,48},{48,64},{64,80},{80,96},{96,112},{112,128},... | collective-permute-start | bytes 786440 | tf_op jit(solution)/shard_map/ppermute | solution.py:24
  48.3 11.3 %collective-permute-start.12 = (f32[27,16,128]{2,1,0:T(8,128)S(1)}, f32[27,16,128]{2,1,0:T(8,128)S(1)}, u32[]{:S(2)}, u32[]{:S(2)}) collective-permute-start(f32[27,16,128]{2,1,0:T(8,128)S(1)} %add.196), channel_id=1, source_target_pairs={{0,16},{16,0},{32,48},{48,32},{64,80},{80,64},{96,112},{112,96},{1... | collective-permute-start | bytes 663560 | tf_op jit(solution)/shard_map/ppermute | solution.py:29
  59.6 14.5 %collective-permute-start.13 = (f32[27,16,128]{2,1,0:T(8,128)S(1)}, f32[27,16,128]{2,1,0:T(8,128)S(1)}, u32[]{:S(2)}, u32[]{:S(2)}) collective-permute-start(f32[27,16,128]{2,1,0:T(8,128)S(1)} %add.197), channel_id=1, source_target_pairs={{0,128},{16,144},{32,160},{48,176},{64,192},{80,208},{96,224},{112... | collective-permute-start | bytes 663560 | tf_op jit(solution)/shard_map/ppermute | solution.py:29
  74.1 12.8 %collective-permute-start.14 = (f32[27,16,128]{2,1,0:T(8,128)S(1)}, f32[27,16,128]{2,1,0:T(8,128)S(1)}, u32[]{:S(2)}, u32[]{:S(2)}) collective-permute-start(f32[27,16,128]{2,1,0:T(8,128)S(1)} %add.198), channel_id=1, source_target_pairs={{0,32},{16,48},{32,0},{48,16},{64,96},{80,112},{96,64},{112,80},{1... | collective-permute-start | bytes 663560 | tf_op jit(solution)/shard_map/ppermute | solution.py:29
  87.0 13.5 %collective-permute-start.15 = (f32[27,16,128]{2,1,0:T(8,128)S(1)}, f32[27,16,128]{2,1,0:T(8,128)S(1)}, u32[]{:S(2)}, u32[]{:S(2)}) collective-permute-start(f32[27,16,128]{2,1,0:T(8,128)S(1)} %add.199), channel_id=1, source_target_pairs={{0,64},{16,80},{32,96},{48,112},{64,0},{80,16},{96,32},{112,48},{1... | collective-permute-start | bytes 663560 | tf_op jit(solution)/shard_map/ppermute | solution.py:29
